TPU v7x, 512 devices: a whole 4x4x16 slice. The times are simulated.
512 devices in a mesh: gx: 64 (over z, y_lo, core), gz: 8 (over x, y_hi).
Axes of the slice: x: 4, y: 4 (y_hi: 2, y_lo: 2; y = y_hi * 2 + y_lo), z: 16, core: 2. Of those that a mesh axis runs over, the one named last changes fastest.
Arguments:
- adjoint: bfloat16 [3, 512, 256, 256], P(None, 'gx', 'gz'), may hold values from -6 to 6
- strain: bfloat16 [512, 256, 256], P('gx', 'gz'), may hold values from -16 to 16
- correction: float32 [256, 256], P('gz'), may hold values from 0.3 to 3
- metric: float32 [256], replicated, may hold values from 0.5 to 4
- stream_inverse: bfloat16 [512, 512], replicated, may hold values from -0.081 to 1.081
- span_inverse: bfloat16 [256, 256], replicated, may hold values from -0.081 to 1.081
- wall_operator: bfloat16 [256, 256], replicated, may hold values from -0.081 to 1.081
Outputs:
- adjoint_next: bfloat16 [3, 512, 256, 256], P(None, 'gx', 'gz')
- gradient: float32 [256, 256], P('gz', 'gx')
All inputs are finite; a program needn't handle non-finite values.
Results may differ from a plain program's by a relative error of at most 0.013.
Values may be sent and summed in bfloat16 or wider, within the bound.
No kernel may reach another device: no remote copies, remote signals or barrier semaphores. Data moves between devices by JAX's collectives and lax.ppermute only.
A program may use at most 64 MiB of HBM per device.

v0:
```python
import jax
import jax.numpy as jnp
from jax import lax
from jax.sharding import PartitionSpec as P

near_coef = 7.0 / 9.0
far_coef = 1.0 / 36.0
time_step = 0.25
f32 = jnp.float32
bf16 = jnp.bfloat16


def stencil(source, axis):
    widened = source.astype(f32)
    near_diff = jnp.roll(widened, -1, axis) - jnp.roll(widened, 1, axis)
    far_diff = jnp.roll(widened, -2, axis) - jnp.roll(widened, 2, axis)
    return (near_coef * near_diff + far_coef * far_diff).astype(bf16)


def derivative(pencil, operator):
    right_side = stencil(pencil, 1)
    product = jnp.einsum("ij,cjp->cip", operator, right_side, preferred_element_type=f32)
    return product.astype(bf16)


def xor_order(blocks, mine):
    size = blocks.shape[0]
    bit = 1
    while bit < size:
        swapped = blocks.reshape(size // (2 * bit), 2, bit, *blocks.shape[1:])[:, ::-1]
        blocks = jnp.where(mine // bit % 2 == 1, swapped.reshape(blocks.shape), blocks)
        bit *= 2
    return blocks


def butterfly(blocks, mine):
    size = blocks.shape[0]
    blocks = xor_order(blocks, mine)
    bit = 1
    while bit < size:
        split = blocks.reshape(size // (2 * bit), 2, bit, *blocks.shape[1:])
        pairs = [(src, src ^ bit) for src in range(size)]
        moved = lax.ppermute(split[:, 1], "gz", pairs)
        blocks = jnp.stack([split[:, 0], moved], axis=1).reshape(blocks.shape)
        bit *= 2
    return xor_order(blocks, mine)


def split_wide(value):
    high = lax.reduce_precision(value, exponent_bits=8, mantissa_bits=7)
    return jnp.stack([high.astype(bf16), (value - high).astype(bf16)])


def join_wide(parts):
    return parts[0].astype(f32) + parts[1].astype(f32)


def row_derivative(pencil, operator):
    right_side = stencil(pencil, 0)
    return jnp.dot(operator, right_side, preferred_element_type=f32).astype(bf16)


def wall_derivative(source, wall_operator, metric):
    product = jnp.einsum("kxzj,ij->kxzi", source, wall_operator, preferred_element_type=f32)
    return product * metric


def on_device(adjoint, strain, correction, metric, stream_inverse, span_inverse, wall_operator):
    comps, nxl, nzl, ny = adjoint.shape
    gxn = lax.axis_size("gx")
    lanes = nzl * ny // gxn
    yparts = ny // lanes
    nx = nxl * gxn
    strain_wide = strain.astype(f32)
    viscosity = (correction[None] * strain_wide).astype(bf16)
    viscous = viscosity.astype(f32)
    xs = jnp.concatenate([adjoint, strain[None]], axis=0)
    xs = xs.reshape(comps + 1, nxl, nzl, yparts, lanes).transpose(2, 3, 1, 0, 4)
    xs = xs.reshape(gxn, nxl, (comps + 1) * lanes)
    xt = lax.all_to_all(xs, "gx", 0, 0, tiled=True).reshape(nx, (comps + 1) * lanes)
    stream_strain = xt[:, comps * lanes :].astype(f32)
    me = lax.axis_index("gx")
    z_at, y_at = (me // yparts, me % yparts)
    corr_row = lax.dynamic_slice(correction, (z_at, y_at * lanes), (1, lanes))
    stream_visc = (corr_row * stream_strain).astype(bf16).astype(f32)
    stream_visc = jnp.tile(stream_visc, (1, comps))
    stream_grad = row_derivative(xt[:, : comps * lanes], stream_inverse)
    stream_flux = (stream_visc * stream_grad.astype(f32)).astype(bf16)
    stream_div = row_derivative(stream_flux, stream_inverse)
    stream_sq = (stream_grad.astype(f32) ** 2).reshape(nx, comps, lanes).sum(axis=1)
    stream_sq = jnp.sum(stream_strain * stream_sq, axis=0)
    z_ids = lax.broadcasted_iota(jnp.int32, (nzl, yparts, lanes), 0)
    y_ids = lax.broadcasted_iota(jnp.int32, (nzl, yparts, lanes), 1)
    owned = (z_ids == z_at) & (y_ids == y_at)
    stream_part = jnp.where(owned, stream_sq[None, None], 0.0).reshape(nzl, ny)
    gzn = lax.axis_size("gz")
    mine = lax.axis_index("gz")
    zs = jnp.concatenate([adjoint, viscosity[None], strain[None]], axis=0)
    zt = lax.all_to_all(zs, "gz", 1, 2, tiled=True)[:, 0]
    span_visc = zt[comps].astype(f32)
    span_strain = zt[comps + 1].astype(f32)
    span_grad = derivative(zt[:comps], span_inverse)
    span_flux = (span_visc[None] * span_grad.astype(f32)).astype(bf16)
    span_div = derivative(span_flux, span_inverse)
    span_sq = jnp.sum(span_strain[None] * span_grad.astype(f32) ** 2, axis=0)
    span_back = jnp.concatenate([span_div, split_wide(span_sq)], axis=0)
    span_back = span_back.reshape(span_back.shape[0], gzn, nzl, ny).transpose(1, 0, 2, 3)
    span_out = butterfly(span_back, mine)
    span_part = jnp.sum(join_wide(span_out[:, comps:].transpose(1, 0, 2, 3)), axis=0)
    span_div = span_out[:, :comps].transpose(1, 0, 2, 3)
    wall_grad = wall_derivative(adjoint, wall_operator, metric).astype(bf16)
    wall_flux = (viscous[None] * wall_grad.astype(f32)).astype(bf16)
    wall_div = wall_derivative(wall_flux, wall_operator, metric)
    wall_part = jnp.sum(strain_wide[None] * wall_grad.astype(f32) ** 2, axis=(0, 1))
    partial_sum = stream_part + span_part + wall_part
    pieces = split_wide(partial_sum.T.reshape(gxn, -1))
    extra = jnp.zeros((gxn, nxl - 2, lanes), bf16)
    extra = jnp.concatenate([pieces[0][:, None], pieces[1][:, None], extra], axis=1)
    back = jnp.concatenate([stream_div.reshape(gxn, nxl, comps * lanes), extra], axis=2)
    back = lax.all_to_all(back, "gx", 0, 0, tiled=True)
    summed = jnp.sum(join_wide(back[:, :2, comps * lanes :].transpose(1, 0, 2)), axis=0)
    summed = summed.reshape(ny // gxn, nzl).T
    back = back[:, :, : comps * lanes].reshape(nzl, yparts, nxl, comps, lanes)
    stream_div = back.transpose(3, 2, 0, 1, 4).reshape(comps, nxl, nzl, ny)
    total = stream_div.astype(f32) + wall_div
    total = total + span_div.astype(f32)
    updated = (adjoint.astype(f32) + time_step * total).astype(bf16)
    gradient = -summed / nx
    return (updated, gradient)


def solution(mesh):
    in_specs = (P(None, "gx", "gz", None), P("gx", "gz", None), P("gz", None), P(), P(), P(), P())
    out_specs = (P(None, "gx", "gz", None), P("gz", "gx"))
    return jax.shard_map(
        on_device, mesh=mesh, in_specs=in_specs, out_specs=out_specs, check_vma=False
    )
```

profile of v0, /device:TPU:8, one launch (start us, length us, event | category | flops | bytes accessed | tf_op | source)
XLA Modules:
  0.0 143.3 jit_solution(535685703489380704)
XLA Ops:
  0.7 1.7 %fusion.47 = (f32[8,32,256]{2,1,0:T(8,128)}, bf16[1,8,32,256]{3,2,0,1:T(8,128)(2,1)S(1)}) fusion(bf16[8,32,256]{2,1,0:T(8,128)(2,1)} %param.8, f32[32,256]{1,0:T(8,128)} %param.9), kind=kLoop, calls=%fused_computation.92 | loop fusion | flops 262144 | bytes 557056 | tf_op jit(solution)/shard_map/convert_element_type | solution.py:76
  2.4 1.8 %pad_maximum_fusion = bf16[5,8,32,256]{3,2,0,1:T(8,128)(2,1)} fusion(bf16[1,8,32,256]{3,2,0,1:T(8,128)(2,1)} %bitcast.145, bf16[1,8,32,256]{3,2,0,1:T(8,128)(2,1)S(1)} %get-tuple-element.50, bf16[3,8,32,256]{3,2,1,0:T(8,128)(2,1)S(1)} %copy-done.1), kind=kLoop, calls=%fused_computation.49 | loop fusion | flops 1966080 | bytes 1310720 | tf_op jit(solution)/shard_map/concatenate | solution.py:98
  4.2 6.0 %all-to-all-start.1 = ((bf16[5,8,32,256]{3,2,0,1:T(8,128)(2,1)}), bf16[5,8,32,256]{3,2,0,1:T(8,128)(2,1)S(1)}, u32[]{:S(2)}, u32[]{:S(2)}) async-start(bf16[5,8,32,256]{3,2,0,1:T(8,128)(2,1)} %pad_maximum_fusion), calls=%async_computation.1 | async-start | bytes 1310720 | tf_op jit(solution)/shard_map/all_to_all | solution.py:99
  10.2 12.1 %all-to-all-done.1 = bf16[5,8,32,256]{3,2,0,1:T(8,128)(2,1)S(1)} async-done(((bf16[5,8,32,256]{3,2,0,1:T(8,128)(2,1)}), bf16[5,8,32,256]{3,2,0,1:T(8,128)(2,1)S(1)}, u32[]{:S(2)}, u32[]{:S(2)}) %all-to-all-start.1) | async-done | bytes 655392 | tf_op jit(solution)/shard_map/all_to_all | solution.py:99
  22.8 0.8 copy-done.6
  23.6 0.5 fusion.29
  24.4 0.5 convolution_convert_fusion
  25.5 3.6 %collective-permute-start = (bf16[4,1,5,32,256]{4,3,0,2,1:T(8,128)(2,1)S(1)}, bf16[4,1,5,32,256]{4,3,0,2,1:T(8,128)(2,1)S(1)}, u32[]{:S(2)}, u32[]{:S(2)}) collective-permute-start(bf16[4,1,5,32,256]{4,3,0,2,1:T(8,128)(2,1)S(1)} %get-tuple-element.36), channel_id=1, source_target_pairs={{0,1},{1,0},{2,3},{3,2},{4,5},{5,4},{6,7},{7,6},{8,9},{9,8},{10,11... | collective-permute-start | bytes 983048 | tf_op jit(solution)/shard_map/ppermute | solution.py:43
  29.3 0.5 copy.48
  29.9 0.8 pad_maximum_fusion.4
  30.8 17.3 %all-to-all-start = ((bf16[64,8,512]{2,1,0:T(8,128)(2,1)}), bf16[64,8,512]{2,1,0:T(8,128)(2,1)}, u32[]{:S(2)}, u32[]{:S(2)}) async-start(bf16[64,8,512]{2,1,0:T(8,128)(2,1)} %bitcast.2), calls=%async_computation | async-start | bytes 1048576 | tf_op jit(solution)/shard_map/all_to_all | solution.py:80
  48.3 2.5 %collective-permute-start.1 = (bf16[2,2,5,32,256]{4,3,1,2,0:T(8,128)(2,1)S(1)}, bf16[2,2,5,32,256]{4,3,1,2,0:T(8,128)(2,1)S(1)}, u32[]{:S(2)}, u32[]{:S(2)}) collective-permute-start(bf16[2,2,5,32,256]{4,3,1,2,0:T(8,128)(2,1)S(1)} %bitcast.154), channel_id=1, source_target_pairs={{0,2},{1,3},{2,0},{3,1},{4,6},{5,7},{6,4},{7,5},{8,10},{9,11},{10,... | collective-permute-start | bytes 983048 | tf_op jit(solution)/shard_map/ppermute | solution.py:43
  50.8 0.5 iota_compare_fusion.1
  51.3 0.6 broadcast_bitcast_fusion
  51.9 8.0 %collective-permute-done.1 = bf16[2,2,5,32,256]{4,3,1,2,0:T(8,128)(2,1)S(1)} collective-permute-done((bf16[2,2,5,32,256]{4,3,1,2,0:T(8,128)(2,1)S(1)}, bf16[2,2,5,32,256]{4,3,1,2,0:T(8,128)(2,1)S(1)}, u32[]{:S(2)}, u32[]{:S(2)}) %collective-permute-start.1) | collective-permute-done | bytes 327712 | tf_op jit(solution)/shard_map/ppermute | solution.py:43
  60.1 2.8 %collective-permute-start.2 = (bf16[1,4,5,32,256]{4,3,1,2,0:T(8,128)(2,1)S(1)}, bf16[1,4,5,32,256]{4,3,1,2,0:T(8,128)(2,1)S(1)}, u32[]{:S(2)}, u32[]{:S(2)}) collective-permute-start(bf16[1,4,5,32,256]{4,3,1,2,0:T(8,128)(2,1)S(1)} %get-tuple-element.32), channel_id=1, source_target_pairs={{0,4},{1,5},{2,6},{3,7},{4,0},{5,1},{6,2},{7,3},{8,12},{9,13},{10,... | collective-permute-start | bytes 983048 | tf_op jit(solution)/shard_map/ppermute | solution.py:43
  63.0 0.8 dynamic-slice_bitcast_fusion
  63.7 1.8 %multiply_reduce_fusion = (f32[32,256]{1,0:T(8,128)}, f32[3,8,32,256]{3,2,1,0:T(8,128)}) fusion(f32[8,32,256]{2,1,0:T(8,128)S(1)} %convert_element_type.211, f32[256]{0:T(256)S(1)} %copy-done.10, bf16[3,8,32,256]{3,2,1,0:T(8,128)(2,1)S(1)} %copy-done.1, bf16[256,256]{1,0:T(8,128)(2,1)S(1)} %copy-done.7), kind=kOutput, calls=%fused_computation.46 | convolution fusion | flops 101834752 | bytes 1606656 | tf_op jit(solution)/shard_map/kxzj,ij->kxzi/dot_general | solution.py:64
  65.5 7.0 %collective-permute-done.2 = bf16[1,4,5,32,256]{4,3,1,2,0:T(8,128)(2,1)S(1)} collective-permute-done((bf16[1,4,5,32,256]{4,3,1,2,0:T(8,128)(2,1)S(1)}, bf16[1,4,5,32,256]{4,3,1,2,0:T(8,128)(2,1)S(1)}, u32[]{:S(2)}, u32[]{:S(2)}) %collective-permute-start.2) | collective-permute-done | bytes 327712 | tf_op jit(solution)/shard_map/ppermute | solution.py:43
  72.6 1.0 maximum_select_fusion
  73.6 1.1 rev.22
  74.7 1.0 select_select_fusion.1
  75.7 1.1 rev.23
  76.8 1.0 select_select_fusion
  77.8 1.0 slice_bitcast_fusion.2
  78.8 0.6 add_reduce_fusion
  79.4 2.2 %all-to-all-done = bf16[64,8,512]{2,1,0:T(8,128)(2,1)} async-done(((bf16[64,8,512]{2,1,0:T(8,128)(2,1)}), bf16[64,8,512]{2,1,0:T(8,128)(2,1)}, u32[]{:S(2)}, u32[]{:S(2)}) %all-to-all-start) | async-done | bytes 524320 | tf_op jit(solution)/shard_map/all_to_all | solution.py:80
  81.6 0.9 slice.224
  82.5 1.0 slice.225
  83.5 0.2 copy.68
  83.7 0.2 fusion.80
  84.0 1.4 fusion.82
  85.3 0.8 fusion.79
  86.1 0.8 fusion.81
  87.1 2.3 %fusion.30 = (f32[512,384]{0,1:T(8,128)S(1)}, f32[512,384]{0,1:T(8,128)S(1)}) fusion(f32[512,128]{0,1:T(8,128)S(1)} %fusion.42, bf16[512,512]{1,0:T(8,128)(2,1)S(1)} %copy-done, f32[1,384]{0,1:T(8,128)} %get-tuple-element.44, f32[511,384]{0,1:T(8,128)} %get-tuple-element.46, f32[511,384]{0,1:T(8,128)} %get-tuple-element.45, ...), kind=kOutput, calls=%fused_computation.64 | convolution fusion | flops 204472320 | bytes 5505024 | tf_op jit(solution)/shard_map/dot_general | solution.py:60
  89.5 0.3 fusion.67
  89.8 0.3 fusion.65
  90.3 0.7 fusion.11
  91.1 0.2 copy.52
  91.6 0.5 copy-done.8
  92.5 0.2 maximum_maximum_fusion
  92.7 44.8 %all_to_all.19 = bf16[64,8,512]{2,1,0:T(8,128)(2,1)S(1)} all-to-all(bf16[64,8,512]{2,1,0:T(8,128)(2,1)S(1)} %maximum_maximum_fusion), channel_id=1, replica_groups=mesh['gx'=64,'gz'=8] {'gx'}, dimensions={0} | all-to-all | bytes 1048576 | tf_op jit(solution)/shard_map/all_to_all | solution.py:120
  137.5 0.8 copy-done.4
  138.3 0.4 copy.76
  138.8 0.6 reshape.254
  139.4 0.9 slice_bitcast_fusion.3
  140.4 0.7 div.47
  141.1 2.2 %fusion.6 = bf16[3,8,32,256]{3,2,1,0:T(8,128)(2,1)} fusion(f32[3,8,32,256]{3,2,1,0:T(8,128)S(1)} %reshape.254, bf16[3,8,32,256]{3,2,1,0:T(8,128)(2,1)S(1)} %copy-done.1, f32[3,8,32,256]{3,2,1,0:T(8,128)S(1)} %copy-done.2, bf16[8,5,32,256]{3,2,0,1:T(8,128)(2,1)} %select_select_fusion, f32[8,32,256]{2,1,0:T(8,128)S(1)} %copy-done.5, f32[256]{0:T(256)S(1)} %copy-done.10, ...), kind=kOutput, calls=%fused_computation.8 | convolution fusion | flops 102629376 | bytes 3146752 | tf_op jit(solution)/shard_map/kxzj,ij->kxzi/dot_general | solution.py:64
  (75 shorter events, 3.1 us)
Async XLA Ops:
  0.6 86.5 %copy-start = (bf16[512,512]{1,0:T(8,128)(2,1)S(1)}, bf16[512,512]{1,0:T(8,128)(2,1)}, u32[]{:S(2)}) copy-start(bf16[512,512]{1,0:T(8,128)(2,1)} %param.11) | copy-start | bytes 1572868
  0.6 1.7 %copy-start.1 = (bf16[3,8,32,256]{3,2,1,0:T(8,128)(2,1)S(1)}, bf16[3,8,32,256]{3,2,1,0:T(8,128)(2,1)}, u32[]{:S(2)}) copy-start(bf16[3,8,32,256]{3,2,1,0:T(8,128)(2,1)} %param.7) | copy-start | bytes 1179652
  4.2 18.1 %all-to-all-start.1 = ((bf16[5,8,32,256]{3,2,0,1:T(8,128)(2,1)}), bf16[5,8,32,256]{3,2,0,1:T(8,128)(2,1)S(1)}, u32[]{:S(2)}, u32[]{:S(2)}) async-start(bf16[5,8,32,256]{3,2,0,1:T(8,128)(2,1)} %pad_maximum_fusion), calls=%async_computation.1 | async-start | bytes 1310720 | tf_op jit(solution)/shard_map/all_to_all | solution.py:99
  22.7 0.9 copy-start.6
  25.4 3.8 %copy-start.3 = (bf16[8,32,256]{2,1,0:T(8,128)(2,1)S(1)}, bf16[8,32,256]{2,1,0:T(8,128)(2,1)}, u32[]{:S(2)}) copy-start(bf16[8,32,256]{2,1,0:T(8,128)(2,1)} %param.8) | copy-start | bytes 393220
  25.5 22.7 %collective-permute-start = (bf16[4,1,5,32,256]{4,3,0,2,1:T(8,128)(2,1)S(1)}, bf16[4,1,5,32,256]{4,3,0,2,1:T(8,128)(2,1)S(1)}, u32[]{:S(2)}, u32[]{:S(2)}) collective-permute-start(bf16[4,1,5,32,256]{4,3,0,2,1:T(8,128)(2,1)S(1)} %get-tuple-element.36), channel_id=1, source_target_pairs={{0,1},{1,0},{2,3},{3,2},{4,5},{5,4},{6,7},{7,6},{8,9},{9,8},{10,11... | collective-permute-start | bytes 983048 | tf_op jit(solution)/shard_map/ppermute | solution.py:43
  30.8 50.8 %all-to-all-start = ((bf16[64,8,512]{2,1,0:T(8,128)(2,1)}), bf16[64,8,512]{2,1,0:T(8,128)(2,1)}, u32[]{:S(2)}, u32[]{:S(2)}) async-start(bf16[64,8,512]{2,1,0:T(8,128)(2,1)} %bitcast.2), calls=%async_computation | async-start | bytes 1048576 | tf_op jit(solution)/shard_map/all_to_all | solution.py:80
  48.3 11.6 %collective-permute-start.1 = (bf16[2,2,5,32,256]{4,3,1,2,0:T(8,128)(2,1)S(1)}, bf16[2,2,5,32,256]{4,3,1,2,0:T(8,128)(2,1)S(1)}, u32[]{:S(2)}, u32[]{:S(2)}) collective-permute-start(bf16[2,2,5,32,256]{4,3,1,2,0:T(8,128)(2,1)S(1)} %bitcast.154), channel_id=1, source_target_pairs={{0,2},{1,3},{2,0},{3,1},{4,6},{5,7},{6,4},{7,5},{8,10},{9,11},{10,... | collective-permute-start | bytes 983048 | tf_op jit(solution)/shard_map/ppermute | solution.py:43
  60.0 3.7 %copy-start.7 = (bf16[256,256]{1,0:T(8,128)(2,1)S(1)}, bf16[256,256]{1,0:T(8,128)(2,1)}, u32[]{:S(2)}) copy-start(bf16[256,256]{1,0:T(8,128)(2,1)} %param.13) | copy-start | bytes 393220
  60.0 3.7 %copy-start.10 = (f32[256]{0:T(256)S(1)}, f32[256]{0:T(256)}, u32[]{:S(2)}) copy-start(f32[256]{0:T(256)} %param.10) | copy-start | bytes 3076
  60.1 12.4 %collective-permute-start.2 = (bf16[1,4,5,32,256]{4,3,1,2,0:T(8,128)(2,1)S(1)}, bf16[1,4,5,32,256]{4,3,1,2,0:T(8,128)(2,1)S(1)}, u32[]{:S(2)}, u32[]{:S(2)}) collective-permute-start(bf16[1,4,5,32,256]{4,3,1,2,0:T(8,128)(2,1)S(1)} %get-tuple-element.32), channel_id=1, source_target_pairs={{0,4},{1,5},{2,6},{3,7},{4,0},{5,1},{6,2},{7,3},{8,12},{9,13},{10,... | collective-permute-start | bytes 983048 | tf_op jit(solution)/shard_map/ppermute | solution.py:43
  91.3 0.8 copy-start.8
  91.3 0.8 copy-start.9
  91.3 0.8 copy-start.11
  91.4 0.8 copy-start.12
  137.5 0.8 copy-start.4
  138.7 2.3 %copy-start.2 = (f32[3,8,32,256]{3,2,1,0:T(8,128)S(1)}, f32[3,8,32,256]{3,2,1,0:T(8,128)}, u32[]{:S(2)}) copy-start(f32[3,8,32,256]{3,2,1,0:T(8,128)} %get-tuple-element.54) | copy-start | bytes 2359300
  138.7 2.3 %copy-start.5 = (f32[8,32,256]{2,1,0:T(8,128)S(1)}, f32[8,32,256]{2,1,0:T(8,128)}, u32[]{:S(2)}) copy-start(f32[8,32,256]{2,1,0:T(8,128)} %get-tuple-element.49) | copy-start | bytes 786436
where the time goes:
time: 144 us; the launch traced here: 143 us
  blocking collectives  44.8 us (31%)
  starting transfers between devices  32.2 us (22%)
  waiting for transfers between devices  29.3 us (20%)
  local copies, waits for them, and re-layouts  17.9 us (12%)
  other arithmetic  9.69 us (7%)
  matrix products  8.05 us (6%)
    all_to_all x1, blocking collectives, on_device(): back = lax.all_to_all(back, 'gx', 0, 0, tiled=True)  44.8 us
    all_to_all x1, starting transfers between devices, on_device(): lax.all_to_all(xs, 'gx', 0, 0, tiled=True).reshape(nx, (comps + 1) * lanes)  17.3 us
    ppermute x3, waiting for transfers between devices, butterfly(): moved = lax.ppermute(split[:, 1], 'gz', pairs)  15 us
    all_to_all x1, waiting for transfers between devices, on_device(): zt = lax.all_to_all(zs, 'gz', 1, 2, tiled=True)[:, 0]  12.1 us
    ppermute x3, starting transfers between devices, butterfly(): moved = lax.ppermute(split[:, 1], 'gz', pairs)  8.91 us
    all_to_all x1, starting transfers between devices, on_device(): zt = lax.all_to_all(zs, 'gz', 1, 2, tiled=True)[:, 0]  6.03 us
    dot_general x2, matrix products, wall_derivative(): jnp.einsum('kxzj,ij->kxzi', source, wall_operator, preferred_element_type...  4.02 us
    select_n x6, other arithmetic, xor_order(): jnp.where(mine // bit % 2 == 1, swapped.reshape(blocks.shape), blocks)  3.1 us
  transfers between devices with their start and end apart: 5, of which 4 were waited for; matrix products, arithmetic and copies ran while one was open for 9% of the time, Pallas kernels for 0%

commit v1 on v0

--- a/solution.py
+++ b/solution.py
@@ -8,6 +8,14 @@
 time_step = 0.25
 f32 = jnp.float32
 bf16 = jnp.bfloat16
+
+
+def mark_files_for(xx):
+    carry_in = lax.axis_size("gz")
+    everything = jnp.split(xx, carry_in, 1)
+    local_next = jnp.stack(everything, axis=0)
+    current_value = lax.all_to_all(local_next, axis_name="gz", split_axis=0, concat_axis=0)
+    return jnp.concatenate(current_value, 2)
 
 
 def stencil(source, axis):
@@ -96,7 +104,7 @@
     gzn = lax.axis_size("gz")
     mine = lax.axis_index("gz")
     zs = jnp.concatenate([adjoint, viscosity[None], strain[None]], axis=0)
-    zt = lax.all_to_all(zs, "gz", 1, 2, tiled=True)[:, 0]
+    zt = mark_files_for(zs)[:, 0]
     span_visc = zt[comps].astype(f32)
     span_strain = zt[comps + 1].astype(f32)
     span_grad = derivative(zt[:comps], span_inverse)

time: 144 us -> 149 us (1.035)
  local copies, waits for them, and re-layouts: 17.9 us -> 24.8 us
  other arithmetic: 9.69 us -> 8.02 us
    unnamed x30 -> x43, local copies, waits for them, and re-layouts: 2.52 us -> 8.04 us
    concatenate x1, other arithmetic: 1.78 us -> 0.08 us  [on_device(): zs = jnp.concatenate([adjoint, viscosity[None], strain[None]], axis=0)]
  transfers between devices with their start and end apart: 5 -> 5, of which waited for: 4 -> 4; matrix products, arithmetic and copies ran while one was open for 9% -> 8% of each run, Pallas kernels for 0% -> 0%
where the time goes in v1:
time: 149 us; the launch traced here: 148 us
  blocking collectives  44.7 us (30%)
  starting transfers between devices  32.2 us (22%)
  waiting for transfers between devices  29.2 us (20%)
  local copies, waits for them, and re-layouts  24.8 us (17%)
  other arithmetic  8.02 us (5%)
  matrix products  7.89 us (5%)
    all_to_all x1, blocking collectives, on_device(): back = lax.all_to_all(back, 'gx', 0, 0, tiled=True)  44.7 us
    all_to_all x1, starting transfers between devices, on_device(): lax.all_to_all(xs, 'gx', 0, 0, tiled=True).reshape(nx, (comps + 1) * lanes)  17.3 us
    ppermute x3, waiting for transfers between devices, butterfly(): moved = lax.ppermute(split[:, 1], 'gz', pairs)  14.9 us
    all_to_all x1, waiting for transfers between devices, mark_files_for(): lax.all_to_all(local_next, axis_name='gz', split_axis=0, concat_axis=0)  12.1 us
    ppermute x3, starting transfers between devices, butterfly(): moved = lax.ppermute(split[:, 1], 'gz', pairs)  8.91 us
    unnamed x43, local copies, waits for them, and re-layouts  8.04 us
    all_to_all x1, starting transfers between devices, mark_files_for(): lax.all_to_all(local_next, axis_name='gz', split_axis=0, concat_axis=0)  6.03 us
    dot_general x2, matrix products, wall_derivative(): jnp.einsum('kxzj,ij->kxzi', source, wall_operator, preferred_element_type...  3.97 us
  transfers between devices with their start and end apart: 5, of which 4 were waited for; matrix products, arithmetic and copies ran while one was open for 8% of the time, Pallas kernels for 0%

profile of v1, /device:TPU:8, one launch (start us, length us, event | category | flops | bytes accessed | tf_op | source)
XLA Modules:
  0.0 148.3 jit_solution(3952512014182737671)
XLA Ops:
  0.7 1.7 %fusion.55 = (f32[8,32,256]{2,1,0:T(8,128)}, bf16[1,8,32,256]{3,2,1,0:T(8,128)(2,1)S(1)}) fusion(bf16[8,32,256]{2,1,0:T(8,128)(2,1)} %param.8, f32[32,256]{1,0:T(8,128)} %param.9), kind=kLoop, calls=%fused_computation.108 | loop fusion | flops 262144 | bytes 557056 | tf_op jit(solution)/shard_map/convert_element_type | solution.py:84
  2.5 0.6 fusion.54
  3.1 0.6 fusion.53
  3.7 0.7 fusion.52
  4.4 0.7 fusion.51
  5.1 0.6 fusion.50
  5.7 0.6 fusion.49
  6.3 0.6 fusion.48
  6.9 0.6 fusion.47
  7.6 6.0 %all-to-all-start.1 = ((bf16[8,5,1,32,256]{4,3,1,2,0:T(8,128)(2,1)}), bf16[8,5,1,32,256]{4,3,1,2,0:T(8,128)(2,1)S(1)}, u32[]{:S(2)}, u32[]{:S(2)}) async-start(bf16[8,5,1,32,256]{4,3,1,2,0:T(8,128)(2,1)} %fusion.47), calls=%async_computation.1 | async-start | bytes 1310720 | tf_op jit(solution)/shard_map/all_to_all | solution.py:17
  13.6 12.1 %all-to-all-done.1 = bf16[8,5,1,32,256]{4,3,1,2,0:T(8,128)(2,1)S(1)} async-done(((bf16[8,5,1,32,256]{4,3,1,2,0:T(8,128)(2,1)}), bf16[8,5,1,32,256]{4,3,1,2,0:T(8,128)(2,1)S(1)}, u32[]{:S(2)}, u32[]{:S(2)}) %all-to-all-start.1) | async-done | bytes 655392 | tf_op jit(solution)/shard_map/all_to_all | solution.py:17
  26.3 0.8 copy-done.8
  27.1 0.5 fusion.29
  28.9 0.8 fusion.85
  29.7 3.6 %collective-permute-start = (bf16[4,1,5,32,256]{4,3,0,2,1:T(8,128)(2,1)}, bf16[4,1,5,32,256]{4,3,0,2,1:T(8,128)(2,1)S(1)}, u32[]{:S(2)}, u32[]{:S(2)}) collective-permute-start(bf16[4,1,5,32,256]{4,3,0,2,1:T(8,128)(2,1)} %get-tuple-element.36), channel_id=1, source_target_pairs={{0,1},{1,0},{2,3},{3,2},{4,5},{5,4},{6,7},{7,6},{8,9},{9,8},{10,11... | collective-permute-start | bytes 983048 | tf_op jit(solution)/shard_map/ppermute | solution.py:51
  34.1 0.9 pad_maximum_fusion.4
  34.9 17.3 %all-to-all-start = ((bf16[64,8,512]{2,1,0:T(8,128)(2,1)}), bf16[64,8,512]{2,1,0:T(8,128)(2,1)}, u32[]{:S(2)}, u32[]{:S(2)}) async-start(bf16[64,8,512]{2,1,0:T(8,128)(2,1)} %bitcast.2), calls=%async_computation | async-start | bytes 1048576 | tf_op jit(solution)/shard_map/all_to_all | solution.py:88
  52.5 2.5 %collective-permute-start.1 = (bf16[2,2,5,32,256]{4,3,1,2,0:T(8,128)(2,1)S(1)}, bf16[2,2,5,32,256]{4,3,1,2,0:T(8,128)(2,1)S(1)}, u32[]{:S(2)}, u32[]{:S(2)}) collective-permute-start(bf16[2,2,5,32,256]{4,3,1,2,0:T(8,128)(2,1)S(1)} %bitcast.203), channel_id=1, source_target_pairs={{0,2},{1,3},{2,0},{3,1},{4,6},{5,7},{6,4},{7,5},{8,10},{9,11},{10,... | collective-permute-start | bytes 983048 | tf_op jit(solution)/shard_map/ppermute | solution.py:51
  55.0 0.6 iota_compare_fusion.1
  55.5 0.6 broadcast_bitcast_fusion
  56.1 7.9 %collective-permute-done.1 = bf16[2,2,5,32,256]{4,3,1,2,0:T(8,128)(2,1)S(1)} collective-permute-done((bf16[2,2,5,32,256]{4,3,1,2,0:T(8,128)(2,1)S(1)}, bf16[2,2,5,32,256]{4,3,1,2,0:T(8,128)(2,1)S(1)}, u32[]{:S(2)}, u32[]{:S(2)}) %collective-permute-start.1) | collective-permute-done | bytes 327712 | tf_op jit(solution)/shard_map/ppermute | solution.py:51
  64.3 2.8 %collective-permute-start.2 = (bf16[1,4,5,32,256]{4,3,1,2,0:T(8,128)(2,1)S(1)}, bf16[1,4,5,32,256]{4,3,1,2,0:T(8,128)(2,1)S(1)}, u32[]{:S(2)}, u32[]{:S(2)}) collective-permute-start(bf16[1,4,5,32,256]{4,3,1,2,0:T(8,128)(2,1)S(1)} %get-tuple-element.32), channel_id=1, source_target_pairs={{0,4},{1,5},{2,6},{3,7},{4,0},{5,1},{6,2},{7,3},{8,12},{9,13},{10,... | collective-permute-start | bytes 983048 | tf_op jit(solution)/shard_map/ppermute | solution.py:51
  67.1 0.8 dynamic-slice_bitcast_fusion
  67.9 1.8 %multiply_reduce_fusion = (f32[32,256]{1,0:T(8,128)}, f32[3,8,32,256]{3,2,1,0:T(8,128)}) fusion(f32[8,32,256]{2,1,0:T(8,128)S(1)} %convert_element_type.211, f32[256]{0:T(256)S(1)} %copy-done.13, bf16[3,8,32,256]{3,2,1,0:T(8,128)(2,1)S(1)} %copy-done.1, bf16[256,256]{1,0:T(8,128)(2,1)S(1)} %copy-done.9), kind=kOutput, calls=%fused_computation.46 | convolution fusion | flops 101834752 | bytes 1606656 | tf_op jit(solution)/shard_map/kxzj,ij->kxzi/dot_general | solution.py:72
  69.7 7.0 %collective-permute-done.2 = bf16[1,4,5,32,256]{4,3,1,2,0:T(8,128)(2,1)S(1)} collective-permute-done((bf16[1,4,5,32,256]{4,3,1,2,0:T(8,128)(2,1)S(1)}, bf16[1,4,5,32,256]{4,3,1,2,0:T(8,128)(2,1)S(1)}, u32[]{:S(2)}, u32[]{:S(2)}) %collective-permute-start.2) | collective-permute-done | bytes 327712 | tf_op jit(solution)/shard_map/ppermute | solution.py:51
  76.8 0.9 maximum_select_fusion
  77.7 1.1 rev.22
  78.9 0.9 select_select_fusion.1
  79.8 1.1 rev.23
  80.9 1.0 select_select_fusion
  81.9 1.0 slice_bitcast_fusion.2
  82.9 0.6 add_reduce_fusion
  83.5 2.2 %all-to-all-done = bf16[64,8,512]{2,1,0:T(8,128)(2,1)} async-done(((bf16[64,8,512]{2,1,0:T(8,128)(2,1)}), bf16[64,8,512]{2,1,0:T(8,128)(2,1)}, u32[]{:S(2)}, u32[]{:S(2)}) %all-to-all-start) | async-done | bytes 524320 | tf_op jit(solution)/shard_map/all_to_all | solution.py:88
  85.7 0.9 slice.223
  86.6 1.0 slice.224
  88.1 1.4 fusion.90
  89.5 0.8 fusion.87
  90.3 0.8 fusion.89
  91.3 0.8 copy-done.6
  92.2 2.2 %fusion.30 = (f32[512,384]{0,1:T(8,128)S(1)}, f32[512,384]{0,1:T(8,128)S(1)}) fusion(f32[512,128]{0,1:T(8,128)S(1)} %fusion.42, bf16[512,512]{1,0:T(8,128)(2,1)S(1)} %copy-done, f32[1,384]{0,1:T(8,128)} %get-tuple-element.44, f32[511,384]{0,1:T(8,128)} %get-tuple-element.46, f32[511,384]{0,1:T(8,128)} %get-tuple-element.45, ...), kind=kOutput, calls=%fused_computation.64 | convolution fusion | flops 204472320 | bytes 5505024 | tf_op jit(solution)/shard_map/dot_general | solution.py:68
  95.3 0.7 fusion.11
  96.5 0.6 copy-done.11
  97.7 44.7 %all_to_all.15 = bf16[64,8,512]{2,1,0:T(8,128)(2,1)S(1)} all-to-all(bf16[64,8,512]{2,1,0:T(8,128)(2,1)S(1)} %maximum_maximum_fusion), channel_id=1, replica_groups=mesh['gx'=64,'gz'=8] {'gx'}, dimensions={0} | all-to-all | bytes 1048576 | tf_op jit(solution)/shard_map/all_to_all | solution.py:128
  142.5 0.8 copy-done.4
  143.7 0.6 reshape.252
  144.4 1.0 slice_bitcast_fusion.11
  145.4 0.7 div.47
  146.1 2.1 %fusion.6 = bf16[3,8,32,256]{3,2,1,0:T(8,128)(2,1)} fusion(f32[3,8,32,256]{3,2,1,0:T(8,128)S(1)} %reshape.252, bf16[3,8,32,256]{3,2,1,0:T(8,128)(2,1)S(1)} %copy-done.1, f32[3,8,32,256]{3,2,1,0:T(8,128)S(1)} %copy-done.2, bf16[8,5,32,256]{3,2,0,1:T(8,128)(2,1)} %select_select_fusion, f32[8,32,256]{2,1,0:T(8,128)S(1)} %copy-done.5, f32[256]{0:T(256)S(1)} %copy-done.13, ...), kind=kOutput, calls=%fused_computation.8 | convolution fusion | flops 102629376 | bytes 3146752 | tf_op jit(solution)/shard_map/kxzj,ij->kxzi/dot_general | solution.py:72
  (89 shorter events, 6.1 us)
Async XLA Ops:
  0.6 90.7 %copy-start = (bf16[512,512]{1,0:T(8,128)(2,1)S(1)}, bf16[512,512]{1,0:T(8,128)(2,1)}, u32[]{:S(2)}) copy-start(bf16[512,512]{1,0:T(8,128)(2,1)} %param.11) | copy-start | bytes 1572868
  0.6 1.7 %copy-start.3 = (bf16[8,32,256]{2,1,0:T(8,128)(2,1)S(1)}, bf16[8,32,256]{2,1,0:T(8,128)(2,1)}, u32[]{:S(2)}) copy-start(bf16[8,32,256]{2,1,0:T(8,128)(2,1)} %param.8) | copy-start | bytes 393220
  0.7 1.7 %copy-start.1 = (bf16[3,8,32,256]{3,2,1,0:T(8,128)(2,1)S(1)}, bf16[3,8,32,256]{3,2,1,0:T(8,128)(2,1)}, u32[]{:S(2)}) copy-start(bf16[3,8,32,256]{3,2,1,0:T(8,128)(2,1)} %param.7) | copy-start | bytes 1179652
  7.6 18.1 %all-to-all-start.1 = ((bf16[8,5,1,32,256]{4,3,1,2,0:T(8,128)(2,1)}), bf16[8,5,1,32,256]{4,3,1,2,0:T(8,128)(2,1)S(1)}, u32[]{:S(2)}, u32[]{:S(2)}) async-start(bf16[8,5,1,32,256]{4,3,1,2,0:T(8,128)(2,1)} %fusion.47), calls=%async_computation.1 | async-start | bytes 1310720 | tf_op jit(solution)/shard_map/all_to_all | solution.py:17
  26.2 0.9 copy-start.8
  29.7 22.7 %collective-permute-start = (bf16[4,1,5,32,256]{4,3,0,2,1:T(8,128)(2,1)}, bf16[4,1,5,32,256]{4,3,0,2,1:T(8,128)(2,1)S(1)}, u32[]{:S(2)}, u32[]{:S(2)}) collective-permute-start(bf16[4,1,5,32,256]{4,3,0,2,1:T(8,128)(2,1)} %get-tuple-element.36), channel_id=1, source_target_pairs={{0,1},{1,0},{2,3},{3,2},{4,5},{5,4},{6,7},{7,6},{8,9},{9,8},{10,11... | collective-permute-start | bytes 983048 | tf_op jit(solution)/shard_map/ppermute | solution.py:51
  34.9 50.8 %all-to-all-start = ((bf16[64,8,512]{2,1,0:T(8,128)(2,1)}), bf16[64,8,512]{2,1,0:T(8,128)(2,1)}, u32[]{:S(2)}, u32[]{:S(2)}) async-start(bf16[64,8,512]{2,1,0:T(8,128)(2,1)} %bitcast.2), calls=%async_computation | async-start | bytes 1048576 | tf_op jit(solution)/shard_map/all_to_all | solution.py:88
  52.5 11.6 %collective-permute-start.1 = (bf16[2,2,5,32,256]{4,3,1,2,0:T(8,128)(2,1)S(1)}, bf16[2,2,5,32,256]{4,3,1,2,0:T(8,128)(2,1)S(1)}, u32[]{:S(2)}, u32[]{:S(2)}) collective-permute-start(bf16[2,2,5,32,256]{4,3,1,2,0:T(8,128)(2,1)S(1)} %bitcast.203), channel_id=1, source_target_pairs={{0,2},{1,3},{2,0},{3,1},{4,6},{5,7},{6,4},{7,5},{8,10},{9,11},{10,... | collective-permute-start | bytes 983048 | tf_op jit(solution)/shard_map/ppermute | solution.py:51
  64.2 3.7 %copy-start.9 = (bf16[256,256]{1,0:T(8,128)(2,1)S(1)}, bf16[256,256]{1,0:T(8,128)(2,1)}, u32[]{:S(2)}) copy-start(bf16[256,256]{1,0:T(8,128)(2,1)} %param.13) | copy-start | bytes 393220
  64.3 3.6 %copy-start.13 = (f32[256]{0:T(256)S(1)}, f32[256]{0:T(256)}, u32[]{:S(2)}) copy-start(f32[256]{0:T(256)} %param.10) | copy-start | bytes 3076
  64.3 12.4 %collective-permute-start.2 = (bf16[1,4,5,32,256]{4,3,1,2,0:T(8,128)(2,1)S(1)}, bf16[1,4,5,32,256]{4,3,1,2,0:T(8,128)(2,1)S(1)}, u32[]{:S(2)}, u32[]{:S(2)}) collective-permute-start(bf16[1,4,5,32,256]{4,3,1,2,0:T(8,128)(2,1)S(1)} %get-tuple-element.32), channel_id=1, source_target_pairs={{0,4},{1,5},{2,6},{3,7},{4,0},{5,1},{6,2},{7,3},{8,12},{9,13},{10,... | collective-permute-start | bytes 983048 | tf_op jit(solution)/shard_map/ppermute | solution.py:51
  91.2 0.9 copy-start.6
  91.2 1.0 copy-start.7
  96.3 0.8 copy-start.11
  96.3 0.8 copy-start.12
  96.5 0.7 copy-start.14
  96.5 0.7 copy-start.15
  142.5 0.8 copy-start.4
  143.7 2.4 %copy-start.2 = (f32[3,8,32,256]{3,2,1,0:T(8,128)S(1)}, f32[3,8,32,256]{3,2,1,0:T(8,128)}, u32[]{:S(2)}) copy-start(f32[3,8,32,256]{3,2,1,0:T(8,128)} %get-tuple-element.54) | copy-start | bytes 2359300
  143.7 2.4 %copy-start.5 = (f32[8,32,256]{2,1,0:T(8,128)S(1)}, f32[8,32,256]{2,1,0:T(8,128)}, u32[]{:S(2)}) copy-start(f32[8,32,256]{2,1,0:T(8,128)} %get-tuple-element.49) | copy-start | bytes 786436
  144.4 1.7 %copy-start.10 = (bf16[256,256]{1,0:T(8,128)(2,1)S(1)}, bf16[256,256]{1,0:T(8,128)(2,1)}, u32[]{:S(2)}) copy-start(bf16[256,256]{1,0:T(8,128)(2,1)} %param.13) | copy-start | bytes 393220
